TPU v7x, 512 devices: a whole 4x8x8 slice. The times are simulated.
512 devices in a mesh: wide: 32 (over z, x), tensor: 16 (over y, core).
Axes of the slice: x: 4, y: 8, z: 8, core: 2. Of those that a mesh axis runs over, the one named last changes fastest.
Arguments:
- tokens: bfloat16 [16384, 8192], P('wide', 'tensor'), may hold values from -6 to 6
- key_value_weight: bfloat16 [8192, 2048], P(None, 'tensor'), may hold values from -0.0625 to 0.0625
- adapter_down_maps: bfloat16 [8192, 512, 64], P('tensor', 'wide'), may hold values from -0.0625 to 0.0625
- adapter_up_maps: bfloat16 [512, 64, 2048], P('wide', None, 'tensor'), may hold values from -0.75 to 0.75
- adapter_per_row: int32 [16384], P('wide'), may hold values from 0 to 511, as said below
- adapter_storage_slot: int32 [512], replicated, may hold values from 0 to 511, as said below
Outputs:
- kv_out: bfloat16 [16384, 2048], P('wide', 'tensor')
Inputs may be any that keep to these rules, and one draw needn't show every extreme that they name: `adapter_per_row`: the adapter stored at position p belongs to owner p // 16 of wide. Among the 512 rows of one index of wide, at most 32 name adapters of one owner; in every draw one owner gets exactly 32 rows from every index of wide. `adapter_storage_slot`: each position is taken by exactly one adapter.
All inputs are finite; a program needn't handle non-finite values.
Results may differ from a plain program's by a relative error of at most 0.0049.
Values may be sent and summed in bfloat16 or wider, within the bound.
No kernel may reach another device: no remote copies, remote signals or barrier semaphores. Data moves between devices by JAX's collectives and lax.ppermute only.
A program may use at most 64 MiB of HBM per device.

v0:
```python
import jax
import jax.numpy as jnp
from jax import lax
from jax.sharding import PartitionSpec as P


def tensor_sum(partial_value, tensor_count):
    position = lax.axis_index("tensor")
    block = partial_value
    steps = []
    step = 1
    while step < tensor_count:
        half = block.shape[0] // 2
        upper = position // step % 2
        low_part = block[:half]
        high_part = block[half:]
        keep = jnp.where(upper == 1, high_part, low_part)
        send = jnp.where(upper == 1, low_part, high_part)
        exchange = [(i, i ^ step) for i in range(tensor_count)]
        block = keep + lax.ppermute(send, "tensor", exchange)
        steps.append((step, upper))
        step *= 2
    block = block.astype(jnp.bfloat16)
    for step, upper in reversed(steps):
        exchange = [(i, i ^ step) for i in range(tensor_count)]
        other = lax.ppermute(block, "tensor", exchange)
        block = jnp.where(
            upper == 1,
            jnp.concatenate([other, block], axis=0),
            jnp.concatenate([block, other], axis=0),
        )
    return block


def body(
    tokens,
    key_value_weight,
    adapter_down_maps,
    adapter_up_maps,
    adapter_per_row,
    adapter_storage_slot,
):
    row_count, feature_portion = tokens.shape
    wide_count = lax.axis_size("wide")
    tensor_count = lax.axis_size("tensor")
    capacity = 2 * row_count // wide_count
    present_adapters = adapter_down_maps.shape[1]
    rank_dimension = adapter_down_maps.shape[2]
    column_portion = key_value_weight.shape[1]
    total_adapters = adapter_storage_slot.shape[0]
    slot_count = wide_count * capacity
    lane = 128
    row_tiles = capacity * feature_portion // lane
    info_rows = 8
    gathered = lax.all_gather(tokens, "tensor", axis=1, tiled=True)
    base_projection_output = jnp.dot(gathered, key_value_weight, preferred_element_type=jnp.float32)
    adapter_match = adapter_per_row[:, None] == jnp.arange(total_adapters, dtype=jnp.int32)[None, :]
    storage_position = jnp.sum(jnp.where(adapter_match, adapter_storage_slot[None, :], 0), axis=1)
    owner_index = storage_position // present_adapters
    local_index = storage_position % present_adapters
    owner_onehot = (
        owner_index[:, None] == jnp.arange(wide_count, dtype=jnp.int32)[None, :]
    ).astype(jnp.float32)
    row_iota = jnp.arange(row_count, dtype=jnp.int32)
    strictly_before = (row_iota[:, None] > row_iota[None, :]).astype(jnp.float32)
    earlier = jnp.dot(strictly_before, owner_onehot, preferred_element_type=jnp.float32)
    rank_in_owner = jnp.sum(earlier * owner_onehot, axis=1).astype(jnp.int32)
    destination = owner_index * capacity + rank_in_owner
    placement = (jnp.arange(slot_count, dtype=jnp.int32)[:, None] == destination[None, :]).astype(
        jnp.bfloat16
    )
    local_code = jnp.broadcast_to(
        (local_index + 1).astype(jnp.bfloat16)[:, None], (row_count, lane)
    )
    extended = jnp.concatenate([tokens, local_code], axis=1)
    placed = jnp.dot(placement, extended, preferred_element_type=jnp.float32).astype(jnp.bfloat16)
    send_rows = placed[:, :feature_portion].reshape(wide_count, row_tiles, lane)
    slot_code = placed[:, feature_portion].reshape(wide_count, 1, capacity)
    slot_code = jnp.pad(slot_code, ((0, 0), (0, info_rows - 1), (0, lane - capacity)))
    send_block = jnp.concatenate([send_rows, slot_code], axis=1)
    got_block = lax.all_to_all(send_block, "wide", split_axis=0, concat_axis=0, tiled=True)
    flat_rows = got_block[:, :row_tiles, :].reshape(slot_count, feature_portion)
    got_code = got_block[:, row_tiles, :capacity].reshape(slot_count).astype(jnp.int32)
    selected = (got_code[:, None] == jnp.arange(1, present_adapters + 1, dtype=jnp.int32)[None, :])[
        :, :, None
    ]
    down_matrix = adapter_down_maps.reshape(feature_portion, present_adapters * rank_dimension)
    all_ranks = jnp.dot(flat_rows, down_matrix, preferred_element_type=jnp.float32)
    all_ranks = all_ranks.reshape(slot_count, present_adapters, rank_dimension)
    partial_value = jnp.sum(jnp.where(selected, all_ranks, 0.0), axis=1)
    ordered = partial_value + 0.0 * gathered[0, 0].astype(jnp.float32)
    scattered = lax.psum_scatter(ordered, "tensor", scatter_dimension=0, tiled=True)
    wide_block = jnp.pad(scattered.astype(jnp.bfloat16), ((0, 0), (0, 448)))
    reduced_rows = lax.all_gather(wide_block, "tensor", axis=0, tiled=True)[:, :64]
    expanded_rows = jnp.where(
        selected, reduced_rows[:, None, :], jnp.zeros((), jnp.bfloat16)
    ).reshape(slot_count, present_adapters * rank_dimension)
    up_matrix = adapter_up_maps.reshape(present_adapters * rank_dimension, column_portion)
    adapter_correction = jnp.dot(
        expanded_rows, up_matrix, preferred_element_type=jnp.float32
    ).astype(jnp.bfloat16)
    adapter_correction = adapter_correction.reshape(wide_count, capacity, column_portion)
    returned_rows = lax.all_to_all(
        adapter_correction, "wide", split_axis=0, concat_axis=0, tiled=True
    )
    returned_rows = returned_rows.reshape(slot_count, column_portion)
    adapter_row_output = jnp.dot(placement.T, returned_rows, preferred_element_type=jnp.float32)
    return (base_projection_output + adapter_row_output).astype(jnp.bfloat16)


def solution(mesh):
    in_specs = (
        P("wide", "tensor"),
        P(None, "tensor"),
        P("tensor", "wide", None),
        P("wide", None, "tensor"),
        P("wide"),
        P(),
    )
    out_specs = P("wide", "tensor")
    return jax.shard_map(body, mesh=mesh, in_specs=in_specs, out_specs=out_specs, check_vma=False)
```

profile of v0, /device:TPU:8, one launch (start us, length us, event | category | flops | bytes accessed | tf_op | source)
XLA Modules:
  0.0 209.3 jit_solution(6343781459754959343)
XLA Ops:
  6.5 0.0 copy-start
  6.5 0.0 all-gather.3.cloned.1.call-start
  6.5 0.7 all-gather.3.cloned.1.call-update
  7.3 0.9 select_reduce_fusion.1
  8.2 0.3 fusion.15
  8.5 0.1 broadcast_in_dim.39
  8.7 2.0 fusion.6
  10.6 0.0 copy-start.1
  10.6 1.2 copy-done.1
  11.8 0.1 slice.24
  11.9 1.3 copy.14
  13.2 1.7 reshape.117
  14.9 0.7 slice_reduce_fusion
  15.6 0.1 reshape_squeeze.5
  15.7 1.2 fusion.16
  16.9 13.2 %all-to-all-start = ((bf16[32,136,128]{2,1,0:T(8,128)(2,1)}), bf16[32,136,128]{2,1,0:T(8,128)(2,1)S(1)}, u32[]{:S(2)}, u32[]{:S(2)}) async-start(bf16[32,136,128]{2,1,0:T(8,128)(2,1)} %fusion.16), calls=%async_computation | async-start | bytes 2228224 | tf_op jit(solution)/shard_map/all_to_all | solution.py:81
  30.1 0.0 reduce-scatter.4.cloned.1.call-start
  30.1 29.4 %all-to-all-done = bf16[32,136,128]{2,1,0:T(8,128)(2,1)S(1)} async-done(((bf16[32,136,128]{2,1,0:T(8,128)(2,1)}), bf16[32,136,128]{2,1,0:T(8,128)(2,1)S(1)}, u32[]{:S(2)}, u32[]{:S(2)}) %all-to-all-start) | async-done | bytes 1114144 | tf_op jit(solution)/shard_map/all_to_all | solution.py:81
  59.5 0.1 fusion.26
  59.6 0.1 reshape.122
  59.6 1.2 slice.27
  60.8 1.7 reshape.123
  62.6 0.1 broadcast_compare_fusion
  62.6 2.6 %select_reduce_fusion = f32[1024,64]{0,1:T(8,128)S(1)} fusion(bf16[1024,512,1]{1,0,2:T(8,128)(2,1)S(1)} %reshape.123, pred[1024,16]{0,1:T(8,128)(4,1)S(1)} %broadcast_compare_fusion, bf16[512,16,64]{0,2,1:T(8,128)(2,1)} %param.8), kind=kOutput, calls=%fused_computation | convolution fusion | flops 1075773440 | bytes 2375680 | tf_op jit(solution)/shard_map/dot_general | solution.py:88
  65.2 0.0 copy-start.2
  65.2 5.7 %all-gather.3.cloned.1.call-done = bf16[512,8192]{1,0:T(8,128)(2,1)} async-done(((bf16[512,512]{1,0:T(8,128)(2,1)}), bf16[512,8192]{1,0:T(8,128)(2,1)}) %all-gather.3.cloned.1.call-update) | async-done | bytes 8388624 | tf_op jit(solution)/shard_map/all_gather | solution.py:55
  70.9 1.2 slice.28
  72.8 1.1 copy.18
  73.8 0.0 reduce-scatter.4.cloned.1.call-update
  73.9 0.0 all-gather.5.cloned.1.call-start
  73.9 56.4 %reduce-scatter.4.cloned.1.call-done = f32[64,64]{1,0:T(8,128)} async-done(((f32[1024,64]{1,0:T(8,128)}), f32[64,64]{1,0:T(8,128)}) %reduce-scatter.4.cloned.1.call-update) | async-done | bytes 16400
  130.3 0.8 copy.19
  131.2 0.1 copy.20
  131.3 0.7 pad.9.clone
  131.9 0.0 all-gather.5.cloned.1.call-update
  131.9 43.3 %all-gather.5.cloned.1.call-done = bf16[1024,512]{1,0:T(8,128)(2,1)} async-done(((bf16[64,512]{1,0:T(8,128)(2,1)}), bf16[1024,512]{1,0:T(8,128)(2,1)}) %all-gather.5.cloned.1.call-update) | async-done | bytes 1048592 | tf_op jit(solution)/shard_map/all_gather | solution.py:94
  175.2 1.0 slice.29
  176.2 0.1 copy.17
  176.3 0.0 copy-done.2
  176.3 1.5 fusion.10
  177.8 10.2 %all-to-all-start.1 = ((bf16[32,32,128]{2,1,0:T(8,128)(2,1)}), bf16[32,32,128]{2,1,0:T(8,128)(2,1)S(1)}, u32[]{:S(2)}, u32[]{:S(2)}) async-start(bf16[32,32,128]{2,1,0:T(8,128)(2,1)} %bitcast.5), calls=%async_computation.1 | async-start | bytes 524288 | tf_op jit(solution)/shard_map/all_to_all | solution.py:103
  188.0 0.0 copy-done
  188.0 5.7 %fusion.32 = f32[512,128]{1,0:T(8,128)S(1)} fusion(bf16[512,8192]{1,0:T(8,128)(2,1)} %all-gather.3.cloned.1.call-done, bf16[8192,128]{1,0:T(8,128)(2,1)S(1)} %copy-done), kind=kOutput, calls=%fused_computation.49 | convolution fusion | flops 1073741824 | bytes 10747904 | tf_op jit(solution)/shard_map/dot_general | solution.py:56
  193.7 7.7 %all-to-all-done.1 = bf16[32,32,128]{2,1,0:T(8,128)(2,1)S(1)} async-done(((bf16[32,32,128]{2,1,0:T(8,128)(2,1)}), bf16[32,32,128]{2,1,0:T(8,128)(2,1)S(1)}, u32[]{:S(2)}, u32[]{:S(2)}) %all-to-all-start.1) | async-done | bytes 262176 | tf_op jit(solution)/shard_map/all_to_all | solution.py:103
  201.4 1.4 fusion.14
  (4 shorter events, 0.0 us)
Async XLA Ops:
  6.5 181.5 %copy-start = (bf16[8192,128]{1,0:T(8,128)(2,1)S(1)}, bf16[8192,128]{1,0:T(8,128)(2,1)}, u32[]{:S(2)}) copy-start(bf16[8192,128]{1,0:T(8,128)(2,1)} %param.7) | copy-start | bytes 6291460
  6.5 64.4 %all-gather.3.cloned.1.call-start = ((), (), s32[]{:S(2)}) async-start(), calls=%async_computation.3 | async-start | bytes 8912896 | tf_op jit(solution)/shard_map/all_gather | solution.py:55
  10.6 1.2 copy-start.1
  16.9 42.6 %all-to-all-start = ((bf16[32,136,128]{2,1,0:T(8,128)(2,1)}), bf16[32,136,128]{2,1,0:T(8,128)(2,1)S(1)}, u32[]{:S(2)}, u32[]{:S(2)}) async-start(bf16[32,136,128]{2,1,0:T(8,128)(2,1)} %fusion.16), calls=%async_computation | async-start | bytes 2228224 | tf_op jit(solution)/shard_map/all_to_all | solution.py:81
  30.1 100.2 %reduce-scatter.4.cloned.1.call-start = ((), (), s32[]{:S(2)}) async-start(), calls=%async_computation.5 | async-start | bytes 557056
  65.2 111.1 %copy-start.2 = (bf16[16,64,128]{2,1,0:T(8,128)(2,1)S(1)}, bf16[16,64,128]{2,1,0:T(8,128)(2,1)}, u32[]{:S(2)}) copy-start(bf16[16,64,128]{2,1,0:T(8,128)(2,1)} %param.9) | copy-start | bytes 786436
  73.9 101.3 %all-gather.5.cloned.1.call-start = ((), (), s32[]{:S(2)}) async-start(), calls=%async_computation.4 | async-start | bytes 1114112 | tf_op jit(solution)/shard_map/all_gather | solution.py:94
  177.8 23.6 %all-to-all-start.1 = ((bf16[32,32,128]{2,1,0:T(8,128)(2,1)}), bf16[32,32,128]{2,1,0:T(8,128)(2,1)S(1)}, u32[]{:S(2)}, u32[]{:S(2)}) async-start(bf16[32,32,128]{2,1,0:T(8,128)(2,1)} %bitcast.5), calls=%async_computation.1 | async-start | bytes 524288 | tf_op jit(solution)/shard_map/all_to_all | solution.py:103
Sparse Core Ops, SparseCore 0:
  9.5 61.3 all-gather.2
  74.0 56.2 reduce-scatter.3
  132.7 42.4 all-gather.4
where the time goes:
time: 210 us; the launch traced here: 209 us
  waiting for transfers between devices  143 us (68%)
  starting transfers between devices  23.4 us (11%)
  between operations  13.9 us (7%)
  matrix products  13.4 us (6%)
  local copies, waits for them, and re-layouts  13.1 us (6%)
  other arithmetic  2.31 us (1%)
    unnamed x4, waiting for transfers between devices  57.2 us
    all_gather x1, waiting for transfers between devices, body(): lax.all_gather(wide_block, 'tensor', axis=0, tiled=True)[:, :64]  43.3 us
    all_to_all x1, waiting for transfers between devices, body(): lax.all_to_all(send_block, 'wide', split_axis=0, concat_axis=0, tiled=True)  29.4 us
    all_to_all x1, starting transfers between devices, body(): lax.all_to_all(send_block, 'wide', split_axis=0, concat_axis=0, tiled=True)  13.2 us
    all_to_all x1, starting transfers between devices, body(): lax.all_to_all(adapter_correction, 'wide', split_axis=0, concat_axis=0, t...  10.2 us
    all_to_all x1, waiting for transfers between devices, body(): lax.all_to_all(adapter_correction, 'wide', split_axis=0, concat_axis=0, t...  7.66 us
    dot_general x1, matrix products, body(): jnp.dot(gathered, key_value_weight, preferred_element_type=jnp.float32)  5.7 us
    all_gather x1, waiting for transfers between devices, body(): gathered = lax.all_gather(tokens, 'tensor', axis=1, tiled=True)  5.69 us
  transfers between devices with their start and end apart: 5, of which 5 were waited for; matrix products, arithmetic and copies ran while one was open for 9% of the time, Pallas kernels for 0%

commit v1 on v0

--- a/solution.py
+++ b/solution.py
@@ -2,6 +2,12 @@
 import jax.numpy as jnp
 from jax import lax
 from jax.sharding import PartitionSpec as P
+
+
+def gather_from_all(x, axis, dim):
+    length = lax.axis_size(axis)
+    repeats = [length if d == dim else 1 for d in range(x.ndim)]
+    return lax.all_to_all(jnp.tile(x, repeats), axis, split_axis=dim, concat_axis=dim, tiled=True)
 
 
 def tensor_sum(partial_value, tensor_count):
@@ -91,7 +97,7 @@
     ordered = partial_value + 0.0 * gathered[0, 0].astype(jnp.float32)
     scattered = lax.psum_scatter(ordered, "tensor", scatter_dimension=0, tiled=True)
     wide_block = jnp.pad(scattered.astype(jnp.bfloat16), ((0, 0), (0, 448)))
-    reduced_rows = lax.all_gather(wide_block, "tensor", axis=0, tiled=True)[:, :64]
+    reduced_rows = gather_from_all(wide_block, "tensor", 0)[:, :64]
     expanded_rows = jnp.where(
         selected, reduced_rows[:, None, :], jnp.zeros((), jnp.bfloat16)
     ).reshape(slot_count, present_adapters * rank_dimension)

time: 210 us -> 202 us (0.962)
  the two profiles are of different devices: /device:TPU:8 before, /device:TPU:1 now
where the time goes in v1:
time: 202 us; the launch traced here: 201 us
  waiting for transfers between devices  101 us (50%)
  blocking collectives  35.2 us (17%)
  starting transfers between devices  23.7 us (12%)
  between operations  14.2 us (7%)
  matrix products  13.4 us (7%)
  local copies, waits for them, and re-layouts  11.7 us (6%)
  other arithmetic  2.31 us (1%)
    unnamed x3, waiting for transfers between devices  56.7 us
    all_to_all x1, blocking collectives, gather_from_all(): lax.all_to_all(jnp.tile(x, repeats), axis, split_axis=dim, concat_axis=di...  35.2 us
    all_to_all x1, waiting for transfers between devices, body(): lax.all_to_all(send_block, 'wide', split_axis=0, concat_axis=0, tiled=True)  27.3 us
    all_to_all x1, starting transfers between devices, body(): lax.all_to_all(send_block, 'wide', split_axis=0, concat_axis=0, tiled=True)  13.7 us
    all_gather x1, waiting for transfers between devices, body(): gathered = lax.all_gather(tokens, 'tensor', axis=1, tiled=True)  9.95 us
    all_to_all x1, starting transfers between devices, body(): lax.all_to_all(adapter_correction, 'wide', split_axis=0, concat_axis=0, t...  9.9 us
    all_to_all x1, waiting for transfers between devices, body(): lax.all_to_all(adapter_correction, 'wide', split_axis=0, concat_axis=0, t...  6.98 us
    dot_general x1, matrix products, body(): jnp.dot(gathered, key_value_weight, preferred_element_type=jnp.float32)  5.7 us
  transfers between devices with their start and end apart: 4, of which 4 were waited for; matrix products, arithmetic and copies ran while one was open for 10% of the time, Pallas kernels for 0%

profile of v1, /device:TPU:1, one launch (start us, length us, event | category | flops | bytes accessed | tf_op | source)
XLA Modules:
  0.0 201.3 jit_solution(17393839653652171530)
XLA Ops:
  6.5 0.0 copy-start
  6.5 0.0 all-gather.2.cloned.1.call-start
  6.5 0.7 all-gather.2.cloned.1.call-update
  7.3 0.9 select_reduce_fusion.1
  8.2 0.3 fusion.15
  8.5 0.1 broadcast_in_dim.39
  8.7 2.0 fusion.6
  10.6 0.0 copy-start.1
  10.6 1.2 copy-done.1
  11.8 0.1 slice.24
  11.9 1.3 copy.19
  13.2 1.7 reshape.124
  14.9 0.7 slice_reduce_fusion
  15.6 0.1 reshape_squeeze.5
  15.7 1.2 fusion.16
  16.9 13.7 %all-to-all-start = ((bf16[32,136,128]{2,1,0:T(8,128)(2,1)}), bf16[32,136,128]{2,1,0:T(8,128)(2,1)S(1)}, u32[]{:S(2)}, u32[]{:S(2)}) async-start(bf16[32,136,128]{2,1,0:T(8,128)(2,1)} %fusion.16), calls=%async_computation | async-start | bytes 2228224 | tf_op jit(solution)/shard_map/all_to_all | solution.py:87
  30.6 0.0 reduce-scatter.4.cloned.1.call-start
  30.7 27.3 %all-to-all-done = bf16[32,136,128]{2,1,0:T(8,128)(2,1)S(1)} async-done(((bf16[32,136,128]{2,1,0:T(8,128)(2,1)}), bf16[32,136,128]{2,1,0:T(8,128)(2,1)S(1)}, u32[]{:S(2)}, u32[]{:S(2)}) %all-to-all-start) | async-done | bytes 1114144 | tf_op jit(solution)/shard_map/all_to_all | solution.py:87
  58.0 0.1 fusion.26
  58.0 0.1 reshape.129
  58.1 1.2 slice.27
  59.3 1.8 reshape.130
  61.1 0.1 broadcast_compare_fusion
  61.2 2.5 %select_reduce_fusion = f32[1024,64]{0,1:T(8,128)S(1)} fusion(bf16[1024,512,1]{1,0,2:T(8,128)(2,1)S(1)} %reshape.130, pred[1024,16]{0,1:T(8,128)(4,1)S(1)} %broadcast_compare_fusion, bf16[512,16,64]{0,2,1:T(8,128)(2,1)} %param.8), kind=kOutput, calls=%fused_computation | convolution fusion | flops 1075773440 | bytes 2375680 | tf_op jit(solution)/shard_map/dot_general | solution.py:94
  63.7 10.0 %all-gather.2.cloned.1.call-done = bf16[512,8192]{1,0:T(8,128)(2,1)} async-done(((bf16[512,512]{1,0:T(8,128)(2,1)}), bf16[512,8192]{1,0:T(8,128)(2,1)}) %all-gather.2.cloned.1.call-update) | async-done | bytes 8388624 | tf_op jit(solution)/shard_map/all_gather | solution.py:61
  73.7 1.2 slice.28
  75.5 1.1 copy.23
  76.6 0.0 reduce-scatter.4.cloned.1.call-update
  76.6 55.9 %reduce-scatter.4.cloned.1.call-done = f32[64,64]{1,0:T(8,128)} async-done(((f32[1024,64]{1,0:T(8,128)}), f32[64,64]{1,0:T(8,128)}) %reduce-scatter.4.cloned.1.call-update) | async-done | bytes 16400
  132.6 0.8 copy.24
  133.4 0.1 copy.25
  133.5 0.0 copy-start.2
  133.5 0.1 tile.2
  133.6 35.2 %all_to_all.19 = bf16[16,64,512]{2,1,0:T(8,128)(2,1)S(1)} all-to-all(bf16[16,64,512]{2,1,0:T(8,128)(2,1)S(1)} %tile.2), channel_id=1, replica_groups=mesh['wide'=32,'tensor'=16] {'tensor'}, dimensions={0} | all-to-all | bytes 2097152 | tf_op jit(solution)/shard_map/all_to_all | solution.py:10
  168.8 0.1 copy.22
  169.0 0.0 copy-done.2
  169.0 1.5 fusion.10
  170.5 9.9 %all-to-all-start.2 = ((bf16[32,32,128]{2,1,0:T(8,128)(2,1)}), bf16[32,32,128]{2,1,0:T(8,128)(2,1)S(1)}, u32[]{:S(2)}, u32[]{:S(2)}) async-start(bf16[32,32,128]{2,1,0:T(8,128)(2,1)} %bitcast.6), calls=%async_computation.2 | async-start | bytes 524288 | tf_op jit(solution)/shard_map/all_to_all | solution.py:109
  180.4 0.0 copy-done
  180.4 5.7 %fusion.32 = f32[512,128]{1,0:T(8,128)S(1)} fusion(bf16[512,8192]{1,0:T(8,128)(2,1)} %all-gather.2.cloned.1.call-done, bf16[8192,128]{1,0:T(8,128)(2,1)S(1)} %copy-done), kind=kOutput, calls=%fused_computation.49 | convolution fusion | flops 1073741824 | bytes 10747904 | tf_op jit(solution)/shard_map/dot_general | solution.py:62
  186.1 7.0 %all-to-all-done.2 = bf16[32,32,128]{2,1,0:T(8,128)(2,1)S(1)} async-done(((bf16[32,32,128]{2,1,0:T(8,128)(2,1)}), bf16[32,32,128]{2,1,0:T(8,128)(2,1)S(1)}, u32[]{:S(2)}, u32[]{:S(2)}) %all-to-all-start.2) | async-done | bytes 262176 | tf_op jit(solution)/shard_map/all_to_all | solution.py:109
  193.1 1.4 fusion.14
  (6 shorter events, 0.1 us)
Async XLA Ops:
  6.5 173.8 %copy-start = (bf16[8192,128]{1,0:T(8,128)(2,1)S(1)}, bf16[8192,128]{1,0:T(8,128)(2,1)}, u32[]{:S(2)}) copy-start(bf16[8192,128]{1,0:T(8,128)(2,1)} %param.7) | copy-start | bytes 6291460
  6.5 67.1 %all-gather.2.cloned.1.call-start = ((), (), s32[]{:S(2)}) async-start(), calls=%async_computation.4 | async-start | bytes 8912896 | tf_op jit(solution)/shard_map/all_gather | solution.py:61
  10.6 1.2 copy-start.1
  16.9 41.1 %all-to-all-start = ((bf16[32,136,128]{2,1,0:T(8,128)(2,1)}), bf16[32,136,128]{2,1,0:T(8,128)(2,1)S(1)}, u32[]{:S(2)}, u32[]{:S(2)}) async-start(bf16[32,136,128]{2,1,0:T(8,128)(2,1)} %fusion.16), calls=%async_computation | async-start | bytes 2228224 | tf_op jit(solution)/shard_map/all_to_all | solution.py:87
  30.6 101.9 %reduce-scatter.4.cloned.1.call-start = ((), (), s32[]{:S(2)}) async-start(), calls=%async_computation.5 | async-start | bytes 557056
  133.5 35.5 %copy-start.2 = (bf16[16,64,128]{2,1,0:T(8,128)(2,1)S(1)}, bf16[16,64,128]{2,1,0:T(8,128)(2,1)}, u32[]{:S(2)}) copy-start(bf16[16,64,128]{2,1,0:T(8,128)(2,1)} %param.9) | copy-start | bytes 786436
  170.5 22.6 %all-to-all-start.2 = ((bf16[32,32,128]{2,1,0:T(8,128)(2,1)}), bf16[32,32,128]{2,1,0:T(8,128)(2,1)S(1)}, u32[]{:S(2)}, u32[]{:S(2)}) async-start(bf16[32,32,128]{2,1,0:T(8,128)(2,1)} %bitcast.6), calls=%async_computation.2 | async-start | bytes 524288 | tf_op jit(solution)/shard_map/all_to_all | solution.py:109
Sparse Core Ops, SparseCore 0:
  9.5 64.1 all-gather.1
  76.7 55.7 reduce-scatter.3
